TPU v7x, 32 devices: a whole 2x2x4 slice. The times are simulated.
32 devices in a mesh: req: 2 (over x), seq: 16 (over z, y, core).
Axes of the slice: x: 2, y: 2, z: 4, core: 2. Of those that a mesh axis runs over, the one named last changes fastest.
Arguments:
- states: bfloat16 [4, 4, 4544], P(None, 'req', 'seq'), may hold values from -6 to 6
- kv_cache: bfloat16 [4, 8192, 128], P('req', 'seq'), may hold values from -48 to 48, as said below
- lengths: int32 [4], replicated, may hold values from 1 to 8188, as said below
- placement: int32 [4], replicated, may hold values from 0 to 3, each once
- norm_gain: bfloat16 [4544], replicated, may hold values from 0.25 to 1.75
- norm_bias: bfloat16 [4544], replicated, may hold values from -1.5 to 1.5
- w_query: bfloat16 [4544, 4544], P('req', 'seq'), may hold values from -0.09375 to 0.09375
- w_keyval: bfloat16 [4544, 128], P('req'), may hold values from -0.09375 to 0.09375
- w_out: bfloat16 [4544, 4544], P('seq', 'req'), may hold values from -0.09375 to 0.09375
- w_up: bfloat16 [4544, 18176], P('req', 'seq'), may hold values from -0.09375 to 0.09375
- w_down: bfloat16 [18176, 4544], P('seq', 'req'), may hold values from -0.046875 to 0.046875
Outputs:
- new_states: bfloat16 [4, 4, 4544], P(None, 'req', 'seq')
- new_cache: bfloat16 [4, 8192, 128], P('req', 'seq')
Inputs may be any that keep to these rules, and one draw needn't show every extreme that they name: Request r's cache holds its first lengths[r] positions; some request has exactly 8188. `kv_cache`: row i is the cache of request placement[i]; positions at or beyond that request's length hold arbitrary values. `placement`: each request is served by exactly one slot.
All inputs are finite; a program needn't handle non-finite values.
Results may differ from a plain program's by a relative error of at most 0.012.
The roundings to bfloat16 on the way count: a program that leaves them out, or rounds other values in their place, can miss the bound.
Values may be sent and summed in bfloat16 or wider, within the bound.
No kernel may reach another device: no remote copies, remote signals or barrier semaphores. Data moves between devices by JAX's collectives and lax.ppermute only.
A program may use at most 192 MiB of HBM per device.

v0:
```python
import jax
import jax.numpy as jnp
from jax import lax
from jax.sharding import PartitionSpec as P

STEPS = 4
EPSILON = 1e-05
NEGATIVE = -1e30


def joined_2(part, axis, combine):
    gathered = jax.tree.map(lambda a: lax.all_gather(a, axis), part)

    def take(source):
        return jax.tree.map(lambda a: lax.dynamic_index_in_dim(a, source, 0, False), gathered)

    return lax.fori_loop(
        1, lax.axis_size(axis), lambda source, state: combine(state, take(source)), take(0)
    )


def layer_norm(row_block, norm_gain, norm_bias):
    values = row_block.astype(jnp.float32)
    average = jnp.mean(values, axis=-1, keepdims=True)
    centered = values - average
    spread = jnp.mean(centered * centered, axis=-1, keepdims=True)
    scaled = centered * lax.rsqrt(spread + EPSILON)
    return (scaled * norm_gain.astype(jnp.float32) + norm_bias.astype(jnp.float32)).astype(
        jnp.bfloat16
    )


def rotate(vectors, positions):
    head_width = vectors.shape[-1]
    half_width = head_width // 2
    frequency = 10000.0 ** (-(jnp.arange(half_width, dtype=jnp.float32) * 2.0) / head_width)
    angles = positions.astype(jnp.float32)[:, None] * frequency[None, :]
    cosine = jnp.concatenate([jnp.cos(angles), jnp.cos(angles)], axis=-1)[:, None, :]
    sine_wave = jnp.concatenate([jnp.sin(angles), jnp.sin(angles)], axis=-1)[:, None, :]
    turned = jnp.concatenate([-vectors[..., half_width:], vectors[..., :half_width]], axis=-1)
    return vectors * cosine + turned * sine_wave


def combine_parts(earlier, later):
    peak_first, total_first, weighted_first = earlier
    peak_second, total_second, weighted_second = later
    peak_score = jnp.maximum(peak_first, peak_second)
    scale_first = jnp.exp(peak_first - peak_score)
    scale_second = jnp.exp(peak_second - peak_score)
    weight_total = total_first * scale_first + total_second * scale_second
    weighted = weighted_first * scale_first[:, :, None] + weighted_second * scale_second[:, :, None]
    return (peak_score, weight_total, weighted)


def shards(
    states,
    kv_cache,
    lengths,
    placement,
    norm_gain,
    norm_bias,
    w_query,
    w_keyval,
    w_out,
    w_up,
    w_down,
):
    group_rows = kv_cache.shape[0]
    seg_length = kv_cache.shape[1]
    head_width = kv_cache.shape[2] // 2
    model_width = norm_gain.shape[0]
    head_count = model_width // head_width
    slice_width = states.shape[2]
    group_index = lax.axis_index("req")
    shard_index = lax.axis_index("seq")
    own_requests = lax.dynamic_slice_in_dim(placement, group_index * group_rows, group_rows, 0)
    slot_lengths = jnp.take(lengths, own_requests)
    every_request = lax.all_gather(states, "req", axis=1, tiled=True)
    own_states = jnp.take(every_request, own_requests, axis=1)
    full_states = lax.all_gather(own_states, "seq", axis=2, tiled=True)
    query_cols, keyval_cols, up_cols, out_rows, down_rows = (
        lax.all_gather(w_query, "req", axis=0, tiled=True),
        lax.all_gather(w_keyval, "req", axis=0, tiled=True),
        lax.all_gather(w_up, "req", axis=0, tiled=True),
        lax.all_gather(w_out, "req", axis=1, tiled=True),
        lax.all_gather(w_down, "req", axis=1, tiled=True),
    )
    first_matrix = jnp.concatenate([query_cols, keyval_cols, up_cols], axis=1)
    second_matrix = jnp.concatenate([out_rows, down_rows], axis=0)
    local_slots = jnp.arange(seg_length, dtype=jnp.int32)
    global_positions = shard_index * seg_length + local_slots
    cache_now = kv_cache
    outputs = []
    for step_index in range(STEPS):
        current = own_states[step_index]
        normed = layer_norm(full_states[step_index], norm_gain, norm_bias)
        first_out = jnp.dot(normed, first_matrix, preferred_element_type=jnp.float32)
        query_part = first_out[:, :slice_width].astype(jnp.bfloat16)
        keyval = first_out[:, slice_width : slice_width + 2 * head_width]
        up_part = first_out[:, slice_width + 2 * head_width :]
        positions = slot_lengths + step_index
        query_all = lax.all_gather(query_part, "seq", axis=1, tiled=True)
        query_rows = rotate(
            query_all.astype(jnp.float32).reshape(group_rows, head_count, head_width), positions
        ).astype(jnp.bfloat16)
        new_key = rotate(keyval[:, None, :head_width], positions)[:, 0, :]
        new_entry = jnp.concatenate([new_key, keyval[:, head_width:]], axis=-1).astype(jnp.bfloat16)
        write_mask = local_slots[None, :] == (positions - shard_index * seg_length)[:, None]
        cache_now = jnp.where(write_mask[:, :, None], new_entry[:, None, :], cache_now)
        key_rows = cache_now[:, :, :head_width]
        value_rows = cache_now[:, :, head_width:]
        scores = jnp.einsum(
            "ghd,gsd->ghs", query_rows, key_rows, preferred_element_type=jnp.float32
        ) * head_width ** (-0.5)
        valid_mask = (global_positions[None, :] <= positions[:, None])[:, None, :]
        highest = jnp.max(jnp.where(valid_mask, scores, NEGATIVE), axis=-1)
        weights = jnp.where(valid_mask, jnp.exp(scores - highest[:, :, None]), 0.0)
        weight_total = jnp.sum(weights, axis=-1)
        weighted = jnp.einsum(
            "ghs,gsd->ghd", weights, value_rows, preferred_element_type=jnp.float32
        )
        peak_score, denominator, numerator = joined_2(
            (highest, weight_total, weighted), "seq", combine_parts
        )
        mixed_all = (
            (numerator / denominator[:, :, None])
            .reshape(group_rows, model_width)
            .astype(jnp.bfloat16)
        )
        mixed_part = lax.dynamic_slice_in_dim(mixed_all, shard_index * slice_width, slice_width, 1)
        hidden = jax.nn.gelu(up_part, approximate=False).astype(jnp.bfloat16)
        joined = jnp.concatenate([mixed_part, hidden], axis=1)
        partial_sum = jnp.dot(joined, second_matrix, preferred_element_type=jnp.float32)
        update = lax.psum_scatter(partial_sum, "seq", scatter_dimension=1, tiled=True)
        outputs.append((current.astype(jnp.float32) + update).astype(jnp.bfloat16))
    stacked = jnp.stack(outputs)
    slot_states = lax.all_gather(stacked, "req", axis=1, tiled=True)
    request_total = placement.shape[0]
    inverse = (
        jnp.zeros((request_total,), jnp.int32)
        .at[placement]
        .set(jnp.arange(request_total, dtype=jnp.int32))
    )
    own_inverse = lax.dynamic_slice_in_dim(inverse, group_index * group_rows, group_rows, 0)
    return (jnp.take(slot_states, own_inverse, axis=1), cache_now)


def solution(mesh):
    in_specs = (
        P(None, "req", "seq"),
        P("req", "seq", None),
        P(),
        P(),
        P(),
        P(),
        P("req", "seq"),
        P("req", None),
        P("seq", "req"),
        P("req", "seq"),
        P("seq", "req"),
    )
    out_specs = (P(None, "req", "seq"), P("req", "seq", None))
    return jax.shard_map(shards, mesh=mesh, in_specs=in_specs, out_specs=out_specs, check_vma=False)
```

profile of v0, /device:TPU:8, one launch (start us, length us, event | category | flops | bytes accessed | tf_op | source)
XLA Modules:
  0.0 748.7 jit_solution(15381080556855086247)
XLA Ops:
  7.2 0.7 all-gather.40.cloned.1.call-update
  8.0 0.7 all-gather.38.cloned.1.call-update
  8.7 0.7 all-gather.32.cloned.1.call-update
  10.0 8.6 %copy.124 = bf16[1136,2272]{0,1:T(8,128)(2,1)} copy(bf16[1136,2272]{1,0:T(8,128)(2,1)} %param.31) | data formatting | bytes 10323968 | tf_op args[10]
  18.7 4.4 all_gather.108
  24.0 30.8 %all_gather.109 = bf16[4,2,4544]{0,1,2:T(2,128)(2,1)S(1)} all-gather(bf16[4,2,284]{0,1,2:T(2,128)(2,1)S(1)} %copy.114), channel_id=1, replica_groups=mesh['req'=2,'seq'=16] {'seq'}, dimensions={2}, use_global_device_ids=true | all-gather | bytes 77248 | tf_op jit(solution)/shard_map/all_gather | solution.py:80
  54.8 10.2 %fusion.177 = (bf16[1,2,4544]{0,1,2:T(2,128)(2,1)S(1)}, bf16[1,2,4544]{0,1,2:T(2,128)(2,1)}, f32[1,2,4544]{0,1,2:T(2,128)}, bf16[1,2,4544]{0,1,2:T(2,128)(2,1)}) fusion(bf16[4,2,4544]{0,1,2:T(2,128)(2,1)S(1)} %all_gather.109), kind=kLoop, calls=%fused_computation.365 | loop fusion | flops 9088 | bytes 163584 | tf_op jit(solution)/shard_map/slice | solution.py:96
  65.0 5.3 fusion.48
  70.3 0.6 fusion.178
  70.9 5.5 copy.138
  77.3 0.6 gather_fusion
  77.9 5.1 copy.167
  84.1 5.1 copy.166
  90.2 0.9 copy.119
  91.1 2.4 copy.165
  95.0 0.6 compare_and_fusion
  95.6 0.7 iota_compare_fusion
  96.3 0.7 iota_compare_fusion.2
  96.9 0.6 dynamic-slice
  98.2 0.7 broadcast_compare_fusion.3
  98.9 0.7 multiply_cosine_fusion.3
  99.6 6.0 copy.123
  105.7 6.1 reshape.547
  111.8 3.0 copy.125
  114.7 3.9 copy.150
  118.7 127.5 %all-gather.34.cloned.1.call-done = bf16[4544,1136]{1,0:T(8,128)(2,1)} async-done(((bf16[2272,1136]{1,0:T(8,128)(2,1)}), bf16[4544,1136]{1,0:T(8,128)(2,1)}) %all-gather.34.cloned.1.call-update) | async-done | bytes 10323984 | tf_op jit(solution)/shard_map/all_gather | solution.py:84
  246.2 25.5 %concatenate.126 = bf16[4544,1548]{1,0:T(8,128)(2,1)} concatenate(bf16[4544,284]{1,0:T(8,128)(2,1)S(1)} %bitcast.276, bf16[4544,128]{1,0:T(8,128)(2,1)} %all-gather.32.cloned.1.call-done, bf16[4544,1136]{1,0:T(8,128)(2,1)} %all-gather.34.cloned.1.call-done), dimensions={1} | concatenate | bytes 28136448 | tf_op jit(solution)/shard_map/concatenate | solution.py:88
  271.8 7.6 %fusion.179 = (bf16[2,1548]{1,0:T(2,128)(2,1)S(1)}, f32[2,1548]{1,0:T(2,128)S(1)}) fusion(bf16[4544,1548]{1,0:T(8,128)(2,1)} %concatenate.126, f32[1,2,4544]{2,1,0:T(2,128)} %copy-done.6, f32[2]{0:T(128)} %add_rsqrt_fusion, f32[2]{0:T(128)} %copy-done.26, f32[4544]{0:T(1024)S(1)} %convert_element_type.189, f32[4544]{0:T(1024)S(1)} %convert_element_type.188), kind=kOutput, calls=%fused_computation.367 | convolution fusion | flops 28184984 | bytes 14159520 | tf_op jit(solution)/shard_map/dot_general | solution.py:97
  279.6 1.8 copy-done.2
  281.4 2.1 fusion.180
  283.8 2.1 fusion.181
  286.3 2.1 fusion.182
  288.6 18.7 %all-gather.23 = bf16[16,284,2]{1,2,0:T(2,128)(2,1)S(1)} all-gather(bf16[1,284,2]{1,2,0:T(2,128)(2,1)S(1)} %slice_bitcast_fusion), channel_id=1, replica_groups=mesh['req'=2,'seq'=16] {'seq'}, dimensions={0}, use_global_device_ids=true | all-gather | bytes 19312 | tf_op jit(solution)/shard_map/all_gather | solution.py:102
  309.5 17.5 %all-gather.20 = bf16[16,284,2]{1,2,0:T(2,128)(2,1)S(1)} all-gather(bf16[1,284,2]{1,2,0:T(2,128)(2,1)S(1)} %slice_bitcast_fusion.1), channel_id=1, replica_groups=mesh['req'=2,'seq'=16] {'seq'}, dimensions={0}, use_global_device_ids=true | all-gather | bytes 19312 | tf_op jit(solution)/shard_map/all_gather | solution.py:102
  328.1 19.0 %all-gather.17 = bf16[16,284,2]{1,2,0:T(2,128)(2,1)S(1)} all-gather(bf16[1,284,2]{1,2,0:T(2,128)(2,1)S(1)} %slice_bitcast_fusion.2), channel_id=1, replica_groups=mesh['req'=2,'seq'=16] {'seq'}, dimensions={0}, use_global_device_ids=true | all-gather | bytes 19312 | tf_op jit(solution)/shard_map/all_gather | solution.py:102
  348.3 17.5 %all-gather.13 = bf16[16,284,2]{1,2,0:T(2,128)(2,1)S(1)} all-gather(bf16[1,284,2]{1,2,0:T(2,128)(2,1)S(1)} %slice_bitcast_fusion.3), channel_id=1, replica_groups=mesh['req'=2,'seq'=16] {'seq'}, dimensions={0}, use_global_device_ids=true | all-gather | bytes 19312 | tf_op jit(solution)/shard_map/all_gather | solution.py:102
  367.0 18.8 %all-gather.24 = f32[16,2,71]{2,1,0:T(2,128)S(1)} all-gather(f32[1,2,71]{2,1,0:T(2,128)S(1)} %bitcast.291), channel_id=11, replica_groups=mesh['req'=2,'seq'=16] {'seq'}, dimensions={0}, use_global_device_ids=true | all-gather | bytes 9656 | tf_op jit(solution)/shard_map/all_gather | solution.py:12
  385.8 17.4 %all-gather.25 = f32[16,2,71]{2,1,0:T(2,128)S(1)} all-gather(f32[1,2,71]{2,1,0:T(2,128)S(1)} %bitcast.295), channel_id=12, replica_groups=mesh['req'=2,'seq'=16] {'seq'}, dimensions={0}, use_global_device_ids=true | all-gather | bytes 9656 | tf_op jit(solution)/shard_map/all_gather | solution.py:12
  403.2 22.0 %all-gather.11 = f32[32,71,64]{1,2,0:T(8,128)S(1)} all-gather(f32[2,71,64]{1,2,0:T(8,128)S(1)} %fusion.18), channel_id=13, replica_groups=mesh['req'=2,'seq'=16] {'seq'}, dimensions={0}, use_global_device_ids=true | all-gather | bytes 617984 | tf_op jit(solution)/shard_map/all_gather | solution.py:12
  425.3 4.4 while.79
  430.0 17.9 %all-gather.21 = f32[16,2,71]{2,1,0:T(2,128)S(1)} all-gather(f32[1,2,71]{2,1,0:T(2,128)S(1)} %bitcast.290), channel_id=8, replica_groups=mesh['req'=2,'seq'=16] {'seq'}, dimensions={0}, use_global_device_ids=true | all-gather | bytes 9656 | tf_op jit(solution)/shard_map/all_gather | solution.py:12
  447.8 18.2 %all-gather.22 = f32[16,2,71]{2,1,0:T(2,128)S(1)} all-gather(f32[1,2,71]{2,1,0:T(2,128)S(1)} %bitcast.294), channel_id=9, replica_groups=mesh['req'=2,'seq'=16] {'seq'}, dimensions={0}, use_global_device_ids=true | all-gather | bytes 9656 | tf_op jit(solution)/shard_map/all_gather | solution.py:12
  466.0 21.3 %all-gather.8 = f32[32,71,64]{1,2,0:T(8,128)S(1)} all-gather(f32[2,71,64]{1,2,0:T(8,128)S(1)} %fusion.16), channel_id=10, replica_groups=mesh['req'=2,'seq'=16] {'seq'}, dimensions={0}, use_global_device_ids=true | all-gather | bytes 617984 | tf_op jit(solution)/shard_map/all_gather | solution.py:12
  487.4 4.4 while.78
  492.0 18.3 %all-gather.18 = f32[16,2,71]{2,1,0:T(2,128)S(1)} all-gather(f32[1,2,71]{2,1,0:T(2,128)S(1)} %bitcast.289), channel_id=5, replica_groups=mesh['req'=2,'seq'=16] {'seq'}, dimensions={0}, use_global_device_ids=true | all-gather | bytes 9656 | tf_op jit(solution)/shard_map/all_gather | solution.py:12
  510.3 17.8 %all-gather.19 = f32[16,2,71]{2,1,0:T(2,128)S(1)} all-gather(f32[1,2,71]{2,1,0:T(2,128)S(1)} %bitcast.293), channel_id=6, replica_groups=mesh['req'=2,'seq'=16] {'seq'}, dimensions={0}, use_global_device_ids=true | all-gather | bytes 9656 | tf_op jit(solution)/shard_map/all_gather | solution.py:12
  528.0 21.7 %all-gather.5 = f32[32,71,64]{1,2,0:T(8,128)S(1)} all-gather(f32[2,71,64]{1,2,0:T(8,128)S(1)} %fusion.14), channel_id=7, replica_groups=mesh['req'=2,'seq'=16] {'seq'}, dimensions={0}, use_global_device_ids=true | all-gather | bytes 617984 | tf_op jit(solution)/shard_map/all_gather | solution.py:12
  549.8 4.4 while.77
  554.5 18.0 %all-gather.14 = f32[16,2,71]{2,1,0:T(2,128)S(1)} all-gather(f32[1,2,71]{2,1,0:T(2,128)S(1)} %bitcast.288), channel_id=2, replica_groups=mesh['req'=2,'seq'=16] {'seq'}, dimensions={0}, use_global_device_ids=true | all-gather | bytes 9656 | tf_op jit(solution)/shard_map/all_gather | solution.py:12
  572.5 18.0 %all-gather.15 = f32[16,2,71]{2,1,0:T(2,128)S(1)} all-gather(f32[1,2,71]{2,1,0:T(2,128)S(1)} %bitcast.292), channel_id=3, replica_groups=mesh['req'=2,'seq'=16] {'seq'}, dimensions={0}, use_global_device_ids=true | all-gather | bytes 9656 | tf_op jit(solution)/shard_map/all_gather | solution.py:12
  590.5 21.5 %all-gather.2 = f32[32,71,64]{1,2,0:T(8,128)S(1)} all-gather(f32[2,71,64]{1,2,0:T(8,128)S(1)} %fusion.12), channel_id=4, replica_groups=mesh['req'=2,'seq'=16] {'seq'}, dimensions={0}, use_global_device_ids=true | all-gather | bytes 617984 | tf_op jit(solution)/shard_map/all_gather | solution.py:12
  612.0 4.4 while.76
  617.7 10.7 %fusion.136 = f32[2,4544]{1,0:T(2,128)} fusion(bf16[2,1136]{1,0:T(2,128)(2,1)S(1)} %fusion.115, bf16[2,284]{1,0:T(2,128)(2,1)S(1)} %constant_dynamic-slice_fusion.8, bf16[1136,4544]{0,1:T(8,128)(2,1)} %all-gather.36.cloned.1.call-done, bf16[284,4544]{0,1:T(8,128)(2,1)} %copy.125), kind=kOutput, calls=%fused_computation.232 | convolution fusion | flops 51631200 | bytes 12946992 | tf_op jit(solution)/shard_map/dot_general | solution.py:133
  628.4 4.8 fusion.132
  633.2 4.8 fusion.128
  638.1 4.8 fusion.124
  642.9 1.8 copy.145
  644.7 88.3 %all-reduce.7.cloned.1.call-done = (f32[2,4544]{1,0:T(2,128)}, f32[2,4544]{1,0:T(2,128)}, f32[2,4544]{1,0:T(2,128)}, f32[2,4544]{1,0:T(2,128)}) async-done(((f32[2,4544]{1,0:T(2,128)}, f32[2,4544]{1,0:T(2,128)}, f32[2,4544]{1,0:T(2,128)}, f32[2,4544]{1,0:T(2,128)}), (f32[2,4544]{1,0:T(2,128)}, f32[2,4544]{1,0:T(2,128)}, f32[2,4544]{1,0:T(2,128)}, f32[2,4544]{1,0:T(2,128)})) %all-reduce.7.cloned.1.call-update) | async-done | bytes 145424
  733.0 0.8 fusion.147
  733.7 0.8 fusion.146
  734.5 0.8 fusion.145
  735.3 0.8 fusion.144
  736.1 4.4 all_gather.143
  741.1 0.6 copy.144
  (470 shorter events, 31.1 us)
Async XLA Ops:
  7.2 70.1 %copy-start = (s32[4]{0:T(128)S(1)}, s32[4]{0:T(128)}, u32[]{:S(2)}) copy-start(s32[4]{0:T(128)} %param.23) | copy-start | bytes 52
  7.2 92.4 %all-gather.40.cloned.1.call-start = ((), (), s32[]{:S(2)}) async-start(), calls=%async_computation.4 | async-start | bytes 3981312 | tf_op jit(solution)/shard_map/all_gather | solution.py:85
  7.9 106.8 %all-gather.38.cloned.1.call-start = ((), (), s32[]{:S(2)}) async-start(), calls=%async_computation.3 | async-start | bytes 3981312 | tf_op jit(solution)/shard_map/all_gather | solution.py:82
  8.7 110.0 %all-gather.32.cloned.1.call-start = ((), (), s32[]{:S(2)}) async-start(), calls=%async_computation | async-start | bytes 1744896 | tf_op jit(solution)/shard_map/all_gather | solution.py:83
  9.4 9.3 %copy-start.25 = (bf16[4,2,284]{2,1,0:T(2,128)(2,1)S(1)}, bf16[4,2,284]{2,1,0:T(2,128)(2,1)}, u32[]{:S(2)}) copy-start(bf16[4,2,284]{2,1,0:T(2,128)(2,1)} %param.21) | copy-start | bytes 13636
  9.4 13.7 %copy-start.46 = (s32[4]{0:T(128)S(1)}, s32[4]{0:T(128)}, u32[]{:S(2)}) copy-start(s32[4]{0:T(128)} %param.24) | copy-start | bytes 52
  9.4 236.8 %all-gather.34.cloned.1.call-start = ((), (), s32[]{:S(2)}) async-start(), calls=%async_computation.1 | async-start | bytes 15704064 | tf_op jit(solution)/shard_map/all_gather | solution.py:84
  10.0 607.7 %all-gather.36.cloned.1.call-start = ((), (), s32[]{:S(2)}) async-start(), calls=%async_computation.2 | async-start | bytes 15704064 | tf_op jit(solution)/shard_map/all_gather | solution.py:86
  18.7 714.3 %all-reduce.7.cloned.1.call-start = ((), (), s32[]{:S(2)}) async-start(), calls=%async_computation.5 | async-start | bytes 294912
  54.8 22.4 %copy-start.19 = (bf16[4544]{0:T(1024)(128)(2,1)S(1)}, bf16[4544]{0:T(1024)(128)(2,1)}, u32[]{:S(2)}) copy-start(bf16[4544]{0:T(1024)(128)(2,1)} %param.26) | copy-start | bytes 27268
  54.8 22.4 %copy-start.20 = (bf16[4544]{0:T(1024)(128)(2,1)S(1)}, bf16[4544]{0:T(1024)(128)(2,1)}, u32[]{:S(2)}) copy-start(bf16[4544]{0:T(1024)(128)(2,1)} %param.25) | copy-start | bytes 27268
  65.0 25.2 %copy-start.11 = (bf16[2,512,128]{2,1,0:T(8,128)(2,1)S(1)}, bf16[2,512,128]{2,1,0:T(8,128)(2,1)}, u32[]{:S(2)}) copy-start(bf16[2,512,128]{2,1,0:T(8,128)(2,1)} %param.22) | copy-start | bytes 786436
  65.0 31.9 %copy-start.48 = (u32[32]{0:T(128)S(1)}, u32[32]{0:T(128)}, u32[]{:S(2)}) copy-start(u32[32]{0:T(128)} %constant.327) | copy-start | bytes 388
  76.4 23.2 %copy-start.6 = (f32[1,2,4544]{2,1,0:T(2,128)}, f32[1,2,4544]{2,1,0:T(2,128)S(1)}, u32[]{:S(2)}) copy-start(f32[1,2,4544]{2,1,0:T(2,128)S(1)} %copy.138) | copy-start | bytes 109060
  76.5 1.5 copy-start.26
  83.1 1.0 copy-start.9
  83.2 6.0 copy-start.31
  89.2 10.4 %copy-start.7 = (bf16[1,2,4544]{2,1,0:T(2,128)(2,1)}, bf16[1,2,4544]{2,1,0:T(2,128)(2,1)S(1)}, u32[]{:S(2)}) copy-start(bf16[1,2,4544]{2,1,0:T(2,128)(2,1)S(1)} %copy.166) | copy-start | bytes 54532
  89.4 4.1 copy-start.29
  93.6 4.6 copy-start.27
  271.8 9.6 %copy-start.2 = (bf16[4544,1548]{1,0:T(8,128)(2,1)S(1)}, bf16[4544,1548]{1,0:T(8,128)(2,1)}, u32[]{:S(2)}) copy-start(bf16[4544,1548]{1,0:T(8,128)(2,1)} %concatenate.126) | copy-start | bytes 42204676
  271.8 9.6 %copy-start.10 = (bf16[1,2,4544]{2,1,0:T(2,128)(2,1)S(1)}, bf16[1,2,4544]{2,1,0:T(2,128)(2,1)}, u32[]{:S(2)}) copy-start(bf16[1,2,4544]{2,1,0:T(2,128)(2,1)} %copy-done.9) | copy-start | bytes 54532
  271.8 9.6 %copy-start.32 = (f32[2]{0:T(128)S(1)}, f32[2]{0:T(128)}, u32[]{:S(2)}) copy-start(f32[2]{0:T(128)} %copy-done.31) | copy-start | bytes 28
  271.8 9.6 %copy-start.43 = (f32[2]{0:T(128)S(1)}, f32[2]{0:T(128)}, u32[]{:S(2)}) copy-start(f32[2]{0:T(128)} %add_rsqrt_fusion.1) | copy-start | bytes 28
  281.4 2.4 copy-start.8
  281.4 2.3 copy-start.30
  281.4 2.3 copy-start.42
  283.7 2.3 copy-start.28
  283.8 2.3 copy-start.41
  286.1 21.5 %copy-start.39 = (f32[2,32]{1,0:T(2,128)S(1)}, f32[2,32]{1,0:T(2,128)}, u32[]{:S(2)}) copy-start(f32[2,32]{1,0:T(2,128)} %get-tuple-element.1017) | copy-start | bytes 772
  286.1 21.5 %copy-start.40 = (f32[2,32]{1,0:T(2,128)S(1)}, f32[2,32]{1,0:T(2,128)}, u32[]{:S(2)}) copy-start(f32[2,32]{1,0:T(2,128)} %get-tuple-element.1018) | copy-start | bytes 772
  286.1 21.6 %copy-start.37 = (f32[2,32]{1,0:T(2,128)S(1)}, f32[2,32]{1,0:T(2,128)}, u32[]{:S(2)}) copy-start(f32[2,32]{1,0:T(2,128)} %get-tuple-element.1015) | copy-start | bytes 772
  286.1 21.6 %copy-start.38 = (f32[2,32]{1,0:T(2,128)S(1)}, f32[2,32]{1,0:T(2,128)}, u32[]{:S(2)}) copy-start(f32[2,32]{1,0:T(2,128)} %get-tuple-element.1016) | copy-start | bytes 772
  286.1 21.8 %copy-start.35 = (f32[2,32]{1,0:T(2,128)S(1)}, f32[2,32]{1,0:T(2,128)}, u32[]{:S(2)}) copy-start(f32[2,32]{1,0:T(2,128)} %get-tuple-element.1013) | copy-start | bytes 772
  286.2 21.8 %copy-start.36 = (f32[2,32]{1,0:T(2,128)S(1)}, f32[2,32]{1,0:T(2,128)}, u32[]{:S(2)}) copy-start(f32[2,32]{1,0:T(2,128)} %get-tuple-element.1014) | copy-start | bytes 772
  286.2 21.9 %copy-start.33 = (f32[2,32]{1,0:T(2,128)S(1)}, f32[2,32]{1,0:T(2,128)}, u32[]{:S(2)}) copy-start(f32[2,32]{1,0:T(2,128)} %get-tuple-element.987) | copy-start | bytes 772
  286.2 21.9 %copy-start.34 = (f32[2,32]{1,0:T(2,128)S(1)}, f32[2,32]{1,0:T(2,128)}, u32[]{:S(2)}) copy-start(f32[2,32]{1,0:T(2,128)} %get-tuple-element.988) | copy-start | bytes 772
  286.2 22.1 %copy-start.5 = (bf16[2,512,128]{1,2,0:T(8,128)(2,1)S(1)}, bf16[2,512,128]{1,2,0:T(8,128)(2,1)}, u32[]{:S(2)}) copy-start(bf16[2,512,128]{1,2,0:T(8,128)(2,1)} %copy.119) | copy-start | bytes 786436
  286.2 22.1 %copy-start.21 = (pred[2,512]{1,0:T(4,128)(4,1)S(1)}, pred[2,512]{1,0:T(4,128)(4,1)}, u32[]{:S(2)}) copy-start(pred[2,512]{1,0:T(4,128)(4,1)} %get-tuple-element.1035) | copy-start | bytes 3076
  286.2 22.0 %copy-start.22 = (pred[2,512]{1,0:T(4,128)(4,1)S(1)}, pred[2,512]{1,0:T(4,128)(4,1)}, u32[]{:S(2)}) copy-start(pred[2,512]{1,0:T(4,128)(4,1)} %get-tuple-element.1036) | copy-start | bytes 3076
  286.2 22.0 %copy-start.23 = (pred[2,512]{1,0:T(4,128)(4,1)S(1)}, pred[2,512]{1,0:T(4,128)(4,1)}, u32[]{:S(2)}) copy-start(pred[2,512]{1,0:T(4,128)(4,1)} %get-tuple-element.1037) | copy-start | bytes 3076
  286.2 22.0 %copy-start.24 = (pred[2,512]{1,0:T(4,128)(4,1)S(1)}, pred[2,512]{1,0:T(4,128)(4,1)}, u32[]{:S(2)}) copy-start(pred[2,512]{1,0:T(4,128)(4,1)} %get-tuple-element.1038) | copy-start | bytes 3076
  286.2 22.3 %copy-start.14 = (pred[2,512]{1,0:T(4,128)(4,1)S(1)}, pred[2,512]{1,0:T(4,128)(4,1)}, u32[]{:S(2)}) copy-start(pred[2,512]{1,0:T(4,128)(4,1)} %get-tuple-element.974) | copy-start | bytes 3076
  286.2 41.0 %copy-start.13 = (pred[2,512]{1,0:T(4,128)(4,1)S(1)}, pred[2,512]{1,0:T(4,128)(4,1)}, u32[]{:S(2)}) copy-start(pred[2,512]{1,0:T(4,128)(4,1)} %get-tuple-element.973) | copy-start | bytes 3076
  286.3 61.2 %copy-start.12 = (pred[2,512]{1,0:T(4,128)(4,1)S(1)}, pred[2,512]{1,0:T(4,128)(4,1)}, u32[]{:S(2)}) copy-start(pred[2,512]{1,0:T(4,128)(4,1)} %get-tuple-element.972) | copy-start | bytes 3076
  308.5 0.7 copy-start.4
  617.6 10.7 %copy-start.3 = (bf16[284,4544]{0,1:T(8,128)(2,1)S(1)}, bf16[284,4544]{0,1:T(8,128)(2,1)}, u32[]{:S(2)}) copy-start(bf16[284,4544]{0,1:T(8,128)(2,1)} %copy.125) | copy-start | bytes 7742980
  617.7 10.7 %copy-start.47 = (bf16[1136,4544]{0,1:T(8,128)(2,1)S(1)}, bf16[1136,4544]{0,1:T(8,128)(2,1)}, u32[]{:S(2)}) copy-start(bf16[1136,4544]{0,1:T(8,128)(2,1)} %all-gather.36.cloned.1.call-done) | copy-start | bytes 30971908
  633.2 108.5 %copy-start.1 = (s32[4]{0:T(128)S(1)}, s32[4]{0:T(128)}, u32[]{:S(2)}) copy-start(s32[4]{0:T(128)} %param.23) | copy-start | bytes 52
  638.0 4.9 copy-start.45
  638.0 94.9 %copy-start.18 = (f32[1,2,284]{2,0,1:T(1,128)S(1)}, f32[1,2,284]{2,0,1:T(1,128)}, u32[]{:S(2)}) copy-start(f32[1,2,284]{2,0,1:T(1,128)} %get-tuple-element.969) | copy-start | bytes 6820
  638.0 95.7 %copy-start.17 = (bf16[1,2,284]{2,0,1:T(2,128)(2,1)S(1)}, bf16[1,2,284]{2,0,1:T(2,128)(2,1)}, u32[]{:S(2)}) copy-start(bf16[1,2,284]{2,0,1:T(2,128)(2,1)} %get-tuple-element.970) | copy-start | bytes 3412
  638.0 96.5 %copy-start.16 = (bf16[1,2,284]{2,0,1:T(2,128)(2,1)S(1)}, bf16[1,2,284]{2,0,1:T(2,128)(2,1)}, u32[]{:S(2)}) copy-start(bf16[1,2,284]{2,0,1:T(2,128)(2,1)} %get-tuple-element.968) | copy-start | bytes 3412
  638.0 97.2 %copy-start.15 = (bf16[1,2,284]{2,0,1:T(2,128)(2,1)S(1)}, bf16[1,2,284]{2,0,1:T(2,128)(2,1)}, u32[]{:S(2)}) copy-start(bf16[1,2,284]{2,0,1:T(2,128)(2,1)} %get-tuple-element.967) | copy-start | bytes 3412
  638.1 102.9 %copy-start.44 = (pred[2]{0:T(512)(128)(4,1)S(1)}, pred[2]{0:T(512)(128)(4,1)}, u32[]{:S(2)}) copy-start(pred[2]{0:T(512)(128)(4,1)} %get-tuple-element.945) | copy-start | bytes 10
Sparse Core Ops, SparseCore 0:
  9.6 40.6 all-gather.39
  51.8 39.3 all-gather.37
  92.8 22.5 all-gather.31
  116.8 129.3 all-gather.33
  247.6 129.3 all-gather.35
  643.0 89.9 all-reduce.6
where the time goes:
time: 757 us; the launch traced here: 749 us
  blocking collectives  343 us (45%)
  waiting for transfers between devices  218 us (29%)
  local copies, waits for them, and re-layouts  89.1 us (12%)
  matrix products  41.4 us (5%)
  other arithmetic  38.8 us (5%)
  between operations  15.8 us (2%)
    all_gather x12, blocking collectives, joined_2(): gathered = jax.tree.map(lambda a: lax.all_gather(a, axis), part)  231 us
    all_gather x1, waiting for transfers between devices, shards(): lax.all_gather(w_up, 'req', axis=0, tiled=True)  128 us
    unnamed x7, waiting for transfers between devices  90.9 us
    all_gather x4, blocking collectives, shards(): query_all = lax.all_gather(query_part, 'seq', axis=1, tiled=True)  72.6 us
    unnamed x114, local copies, waits for them, and re-layouts  40.2 us
    all_gather x1, blocking collectives, shards(): full_states = lax.all_gather(own_states, 'seq', axis=2, tiled=True)  30.8 us
    concatenate x1, local copies, waits for them, and re-layouts, shards(): first_matrix = jnp.concatenate([query_cols, keyval_cols, up_cols], axis=1)  25.5 us
    dot_general x4, matrix products, shards(): jnp.dot(joined, second_matrix, preferred_element_type=jnp.float32)  25.1 us
  transfers between devices with their start and end apart: 6, of which 2 were waited for; matrix products, arithmetic and copies ran while one was open for 18% of the time, Pallas kernels for 0%

commit v1 on v0

--- a/solution.py
+++ b/solution.py
@@ -99,7 +99,18 @@
         keyval = first_out[:, slice_width : slice_width + 2 * head_width]
         up_part = first_out[:, slice_width + 2 * head_width :]
         positions = slot_lengths + step_index
-        query_all = lax.all_gather(query_part, "seq", axis=1, tiled=True)
+        ways = lax.axis_size("seq")
+        up = [(d, (d + 1) % ways) for d in range(ways)]
+        down = [(d, (d - 1) % ways) for d in range(ways)]
+        earlier_2, later_2 = ([query_part], [query_part])
+        for _ in range(ways // 2):
+            earlier_2.append(lax.ppermute(earlier_2[-1], "seq", up))
+        for _ in range((ways - 1) // 2):
+            later_2.append(lax.ppermute(later_2[-1], "seq", down))
+        line = jnp.concatenate([*earlier_2[::-1], *later_2[1:]], axis=1)
+        query_all = jnp.roll(
+            line, (lax.axis_index("seq") - ways // 2) * query_part.shape[1], axis=1
+        )
         query_rows = rotate(
             query_all.astype(jnp.float32).reshape(group_rows, head_count, head_width), positions
         ).astype(jnp.bfloat16)

time: 757 us -> 802 us (1.059)
  starting transfers between devices: 0.23 us -> 110 us
  blocking collectives: 343 us -> 276 us
    ppermute x0 -> x60, starting transfers between devices: none -> 110 us  [the longest x28 109 us: shards(): later_2.append(lax.ppermute(later_2[-1], 'seq', down))]
    all_gather x4 -> x0, blocking collectives: 72.6 us -> none  [shards(): query_all = lax.all_gather(query_part, 'seq', axis=1, tiled=True)]
  transfers between devices with their start and end apart: 6 -> 66, of which waited for: 2 -> 4; matrix products, arithmetic and copies ran while one was open for 18% -> 18% of each run, Pallas kernels for 0% -> 0%
where the time goes in v1:
time: 802 us; the launch traced here: 796 us
  blocking collectives  276 us (34%)
  waiting for transfers between devices  222 us (28%)
  starting transfers between devices  110 us (14%)
  local copies, waits for them, and re-layouts  88.6 us (11%)
  matrix products  41.3 us (5%)
  other arithmetic  40.5 us (5%)
  between operations  16.4 us (2%)
    all_gather x12, blocking collectives, joined_2(): gathered = jax.tree.map(lambda a: lax.all_gather(a, axis), part)  236 us
    all_gather x1, waiting for transfers between devices, shards(): lax.all_gather(w_up, 'req', axis=0, tiled=True)  127 us
    ppermute x28, starting transfers between devices, shards(): later_2.append(lax.ppermute(later_2[-1], 'seq', down))  109 us
    unnamed x7, waiting for transfers between devices  91.3 us
    unnamed x114, local copies, waits for them, and re-layouts  39.1 us
    all_gather x1, blocking collectives, shards(): full_states = lax.all_gather(own_states, 'seq', axis=2, tiled=True)  30.8 us
    concatenate x1, local copies, waits for them, and re-layouts, shards(): first_matrix = jnp.concatenate([query_cols, keyval_cols, up_cols], axis=1)  25.6 us
    dot_general x4, matrix products, shards(): jnp.dot(joined, second_matrix, preferred_element_type=jnp.float32)  25 us
  transfers between devices with their start and end apart: 66, of which 4 were waited for; matrix products, arithmetic and copies ran while one was open for 18% of the time, Pallas kernels for 0%

profile of v1, /device:TPU:8, one launch (start us, length us, event | category | flops | bytes accessed | tf_op | source)
XLA Modules:
  0.0 796.1 jit_solution(14250210740742902634)
XLA Ops:
  10.0 8.6 %copy.93 = bf16[1136,2272]{0,1:T(8,128)(2,1)} copy(bf16[1136,2272]{1,0:T(8,128)(2,1)} %param.33) | data formatting | bytes 10323968 | tf_op args[10]
  18.7 4.4 all_gather.96
  24.0 30.8 %all_gather.97 = bf16[4,2,4544]{0,1,2:T(2,128)(2,1)S(1)} all-gather(bf16[4,2,284]{0,1,2:T(2,128)(2,1)S(1)} %copy.84), channel_id=1, replica_groups=mesh['req'=2,'seq'=16] {'seq'}, dimensions={2}, use_global_device_ids=true | all-gather | bytes 77248 | tf_op jit(solution)/shard_map/all_gather | solution.py:80
  54.8 10.2 %fusion.185 = (bf16[1,2,4544]{0,1,2:T(2,128)(2,1)S(1)}, bf16[1,2,4544]{0,1,2:T(2,128)(2,1)}, f32[1,2,4544]{0,1,2:T(2,128)}, bf16[1,2,4544]{0,1,2:T(2,128)(2,1)}) fusion(bf16[4,2,4544]{0,1,2:T(2,128)(2,1)S(1)} %all_gather.97), kind=kLoop, calls=%fused_computation.373 | loop fusion | flops 9088 | bytes 163584 | tf_op jit(solution)/shard_map/slice | solution.py:96
  65.0 5.3 fusion.48
  70.9 5.5 copy.105
  77.9 5.1 copy.133
  84.0 5.1 copy.132
  100.2 6.0 copy.92
  106.2 5.7 reshape.545
  111.9 3.0 copy.94
  114.9 3.9 copy.116
  118.9 127.4 %all-gather.30.cloned.1.call-done = bf16[4544,1136]{1,0:T(8,128)(2,1)} async-done(((bf16[2272,1136]{1,0:T(8,128)(2,1)}), bf16[4544,1136]{1,0:T(8,128)(2,1)}) %all-gather.30.cloned.1.call-update) | async-done | bytes 10323984 | tf_op jit(solution)/shard_map/all_gather | solution.py:84
  246.2 25.6 %concatenate.141 = bf16[4544,1548]{1,0:T(8,128)(2,1)} concatenate(bf16[4544,284]{1,0:T(8,128)(2,1)S(1)} %bitcast.248, bf16[4544,128]{1,0:T(8,128)(2,1)} %all-gather.28.cloned.1.call-done, bf16[4544,1136]{1,0:T(8,128)(2,1)} %all-gather.30.cloned.1.call-done), dimensions={1} | concatenate | bytes 28136448 | tf_op jit(solution)/shard_map/concatenate | solution.py:88
  271.8 7.6 fusion.187
  286.3 2.8 collective-permute-start.53
  295.0 2.6 collective-permute-start.8
  300.4 2.6 collective-permute-start.39
  303.2 2.6 collective-permute-start.54
  305.8 2.6 collective-permute-start.9
  308.5 2.6 collective-permute-start.24
  311.2 3.5 collective-permute-start.40
  314.7 4.5 collective-permute-start.55
  319.3 4.4 collective-permute-start.10
  323.7 4.4 collective-permute-start.25
  328.1 4.4 collective-permute-start.41
  332.6 4.4 collective-permute-start.56
  337.1 4.5 collective-permute-start.11
  341.8 4.4 collective-permute-start.26
  346.1 4.4 collective-permute-start.42
  350.6 4.4 collective-permute-start.57
  355.2 4.4 collective-permute-start.12
  359.6 4.5 collective-permute-start.27
  364.3 4.4 collective-permute-start.43
  368.7 4.4 collective-permute-start.58
  373.4 4.4 collective-permute-start.13
  377.8 4.4 collective-permute-start.44
  382.3 4.4 collective-permute-start.28
  386.8 4.4 collective-permute-start.59
  391.8 4.5 collective-permute-start.14
  396.3 4.4 collective-permute-start.29
  403.5 2.8 collective-permute-done.7
  408.1 24.3 %all-gather.20 = f32[16,2,71]{2,1,0:T(2,128)S(1)} all-gather(f32[1,2,71]{2,1,0:T(2,128)S(1)} %bitcast.258), channel_id=11, replica_groups=mesh['req'=2,'seq'=16] {'seq'}, dimensions={0}, use_global_device_ids=true | all-gather | bytes 9656 | tf_op jit(solution)/shard_map/all_gather | solution.py:12
  432.4 17.5 %all-gather.21 = f32[16,2,71]{2,1,0:T(2,128)S(1)} all-gather(f32[1,2,71]{2,1,0:T(2,128)S(1)} %bitcast.262), channel_id=12, replica_groups=mesh['req'=2,'seq'=16] {'seq'}, dimensions={0}, use_global_device_ids=true | all-gather | bytes 9656 | tf_op jit(solution)/shard_map/all_gather | solution.py:12
  449.9 22.0 %all-gather.11 = f32[32,71,64]{1,2,0:T(8,128)S(1)} all-gather(f32[2,71,64]{1,2,0:T(8,128)S(1)} %fusion.18), channel_id=13, replica_groups=mesh['req'=2,'seq'=16] {'seq'}, dimensions={0}, use_global_device_ids=true | all-gather | bytes 617984 | tf_op jit(solution)/shard_map/all_gather | solution.py:12
  472.0 4.4 while.79
  476.4 17.9 %all-gather.18 = f32[16,2,71]{2,1,0:T(2,128)S(1)} all-gather(f32[1,2,71]{2,1,0:T(2,128)S(1)} %bitcast.257), channel_id=8, replica_groups=mesh['req'=2,'seq'=16] {'seq'}, dimensions={0}, use_global_device_ids=true | all-gather | bytes 9656 | tf_op jit(solution)/shard_map/all_gather | solution.py:12
  494.3 18.1 %all-gather.19 = f32[16,2,71]{2,1,0:T(2,128)S(1)} all-gather(f32[1,2,71]{2,1,0:T(2,128)S(1)} %bitcast.261), channel_id=9, replica_groups=mesh['req'=2,'seq'=16] {'seq'}, dimensions={0}, use_global_device_ids=true | all-gather | bytes 9656 | tf_op jit(solution)/shard_map/all_gather | solution.py:12
  512.4 21.3 %all-gather.8 = f32[32,71,64]{1,2,0:T(8,128)S(1)} all-gather(f32[2,71,64]{1,2,0:T(8,128)S(1)} %fusion.16), channel_id=10, replica_groups=mesh['req'=2,'seq'=16] {'seq'}, dimensions={0}, use_global_device_ids=true | all-gather | bytes 617984 | tf_op jit(solution)/shard_map/all_gather | solution.py:12
  533.9 4.4 while.78
  538.3 18.2 %all-gather.16 = f32[16,2,71]{2,1,0:T(2,128)S(1)} all-gather(f32[1,2,71]{2,1,0:T(2,128)S(1)} %bitcast.256), channel_id=5, replica_groups=mesh['req'=2,'seq'=16] {'seq'}, dimensions={0}, use_global_device_ids=true | all-gather | bytes 9656 | tf_op jit(solution)/shard_map/all_gather | solution.py:12
  556.5 17.8 %all-gather.17 = f32[16,2,71]{2,1,0:T(2,128)S(1)} all-gather(f32[1,2,71]{2,1,0:T(2,128)S(1)} %bitcast.260), channel_id=6, replica_groups=mesh['req'=2,'seq'=16] {'seq'}, dimensions={0}, use_global_device_ids=true | all-gather | bytes 9656 | tf_op jit(solution)/shard_map/all_gather | solution.py:12
  574.4 21.6 %all-gather.5 = f32[32,71,64]{1,2,0:T(8,128)S(1)} all-gather(f32[2,71,64]{1,2,0:T(8,128)S(1)} %fusion.14), channel_id=7, replica_groups=mesh['req'=2,'seq'=16] {'seq'}, dimensions={0}, use_global_device_ids=true | all-gather | bytes 617984 | tf_op jit(solution)/shard_map/all_gather | solution.py:12
  596.1 4.4 while.77
  601.9 21.6 %all-gather.2 = f32[32,71,64]{1,2,0:T(8,128)S(1)} all-gather(f32[2,71,64]{1,2,0:T(8,128)S(1)} %fusion.12), channel_id=4, replica_groups=mesh['req'=2,'seq'=16] {'seq'}, dimensions={0}, use_global_device_ids=true | all-gather | bytes 617984 | tf_op jit(solution)/shard_map/all_gather | solution.py:12
  623.6 18.1 %all-gather.13 = f32[16,2,71]{2,1,0:T(2,128)S(1)} all-gather(f32[1,2,71]{2,1,0:T(2,128)S(1)} %bitcast.259), channel_id=2, replica_groups=mesh['req'=2,'seq'=16] {'seq'}, dimensions={0}, use_global_device_ids=true | all-gather | bytes 9656 | tf_op jit(solution)/shard_map/all_gather | solution.py:12
  641.9 17.7 %all-gather.14 = f32[16,2,71]{2,1,0:T(2,128)S(1)} all-gather(f32[1,2,71]{2,1,0:T(2,128)S(1)} %bitcast.263), channel_id=3, replica_groups=mesh['req'=2,'seq'=16] {'seq'}, dimensions={0}, use_global_device_ids=true | all-gather | bytes 9656 | tf_op jit(solution)/shard_map/all_gather | solution.py:12
  659.6 4.4 while.76
  664.5 10.6 %fusion.144 = f32[2,4544]{1,0:T(2,128)} fusion(bf16[2,1136]{1,0:T(2,128)(2,1)S(1)} %copy-done.33, bf16[2,284]{1,0:T(2,128)(2,1)S(1)} %constant_dynamic-slice_fusion.8, bf16[1136,4544]{0,1:T(8,128)(2,1)} %all-gather.32.cloned.1.call-done, bf16[284,4544]{0,1:T(8,128)(2,1)} %copy.94), kind=kOutput, calls=%fused_computation.244 | convolution fusion | flops 51631200 | bytes 12946992 | tf_op jit(solution)/shard_map/dot_general | solution.py:144
  675.2 4.8 fusion.140
  680.0 4.8 fusion.136
  684.8 4.8 fusion.132
  691.5 88.7 %all-reduce.7.cloned.1.call-done = (f32[2,4544]{1,0:T(2,128)}, f32[2,4544]{1,0:T(2,128)}, f32[2,4544]{1,0:T(2,128)}, f32[2,4544]{1,0:T(2,128)}) async-done(((f32[2,4544]{1,0:T(2,128)}, f32[2,4544]{1,0:T(2,128)}, f32[2,4544]{1,0:T(2,128)}, f32[2,4544]{1,0:T(2,128)}), (f32[2,4544]{1,0:T(2,128)}, f32[2,4544]{1,0:T(2,128)}, f32[2,4544]{1,0:T(2,128)}, f32[2,4544]{1,0:T(2,128)})) %all-reduce.7.cloned.1.call-update) | async-done | bytes 145424
  783.2 4.4 all_gather.127
  (588 shorter events, 62.9 us)
Async XLA Ops:
  7.2 93.0 %all-gather.36.cloned.1.call-start = ((), (), s32[]{:S(2)}) async-start(), calls=%async_computation.4 | async-start | bytes 3981312 | tf_op jit(solution)/shard_map/all_gather | solution.py:85
  7.9 107.0 %all-gather.34.cloned.1.call-start = ((), (), s32[]{:S(2)}) async-start(), calls=%async_computation.3 | async-start | bytes 3981312 | tf_op jit(solution)/shard_map/all_gather | solution.py:82
  8.7 110.2 %all-gather.28.cloned.1.call-start = ((), (), s32[]{:S(2)}) async-start(), calls=%async_computation | async-start | bytes 1744896 | tf_op jit(solution)/shard_map/all_gather | solution.py:83
  9.4 236.8 %all-gather.30.cloned.1.call-start = ((), (), s32[]{:S(2)}) async-start(), calls=%async_computation.1 | async-start | bytes 15704064 | tf_op jit(solution)/shard_map/all_gather | solution.py:84
  10.0 654.5 %all-gather.32.cloned.1.call-start = ((), (), s32[]{:S(2)}) async-start(), calls=%async_computation.2 | async-start | bytes 15704064 | tf_op jit(solution)/shard_map/all_gather | solution.py:86
  18.6 761.5 %all-reduce.7.cloned.1.call-start = ((), (), s32[]{:S(2)}) async-start(), calls=%async_computation.5 | async-start | bytes 294912
  283.6 11.5 %collective-permute-start.30 = (bf16[2,284]{1,0:T(2,128)(2,1)S(1)}, bf16[2,284]{1,0:T(2,128)(2,1)S(1)}, u32[]{:S(2)}, u32[]{:S(2)}) collective-permute-start(bf16[2,284]{1,0:T(2,128)(2,1)S(1)} %slice.278), channel_id=1, source_target_pairs={{0,1},{1,2},{2,3},{3,4},{4,5},{5,6},{6,7},{7,8},{8,9},{9,10},{10,1... | collective-permute-start | bytes 3416 | tf_op jit(solution)/shard_map/ppermute | solution.py:107
  283.6 14.1 %collective-permute-start.38 = (bf16[2,284]{1,0:T(2,128)(2,1)S(1)}, bf16[2,284]{1,0:T(2,128)(2,1)S(1)}, u32[]{:S(2)}, u32[]{:S(2)}) collective-permute-start(bf16[2,284]{1,0:T(2,128)(2,1)S(1)} %slice.278), channel_id=1, source_target_pairs={{0,15},{1,0},{2,1},{3,2},{4,3},{5,4},{6,5},{7,6},{8,7},{9,8},{10,9... | collective-permute-start | bytes 3416 | tf_op jit(solution)/shard_map/ppermute | solution.py:109
  286.3 11.5 %collective-permute-start.45 = (bf16[2,284]{1,0:T(2,128)(2,1)S(1)}, bf16[2,284]{1,0:T(2,128)(2,1)S(1)}, u32[]{:S(2)}, u32[]{:S(2)}) collective-permute-start(bf16[2,284]{1,0:T(2,128)(2,1)S(1)} %slice.291), channel_id=1, source_target_pairs={{0,1},{1,2},{2,3},{3,4},{4,5},{5,6},{6,7},{7,8},{8,9},{9,10},{10,1... | collective-permute-start | bytes 3416 | tf_op jit(solution)/shard_map/ppermute | solution.py:107
  286.3 14.2 %collective-permute-start.53 = (bf16[2,284]{1,0:T(2,128)(2,1)S(1)}, bf16[2,284]{1,0:T(2,128)(2,1)S(1)}, u32[]{:S(2)}, u32[]{:S(2)}) collective-permute-start(bf16[2,284]{1,0:T(2,128)(2,1)S(1)} %slice.291), channel_id=1, source_target_pairs={{0,15},{1,0},{2,1},{3,2},{4,3},{5,4},{6,5},{7,6},{8,7},{9,8},{10,9... | collective-permute-start | bytes 3416 | tf_op jit(solution)/shard_map/ppermute | solution.py:109
  294.6 5.8 collective-permute-start
  295.0 8.0 %collective-permute-start.8 = (bf16[2,284]{1,0:T(2,128)(2,1)S(1)}, bf16[2,284]{1,0:T(2,128)(2,1)S(1)}, u32[]{:S(2)}, u32[]{:S(2)}) collective-permute-start(bf16[2,284]{1,0:T(2,128)(2,1)S(1)} %slice.252), channel_id=1, source_target_pairs={{0,15},{1,0},{2,1},{3,2},{4,3},{5,4},{6,5},{7,6},{8,7},{9,8},{10,9... | collective-permute-start | bytes 3416 | tf_op jit(solution)/shard_map/ppermute | solution.py:109
  297.8 5.4 collective-permute-start.15
  297.8 8.0 %collective-permute-start.23 = (bf16[2,284]{1,0:T(2,128)(2,1)S(1)}, bf16[2,284]{1,0:T(2,128)(2,1)S(1)}, u32[]{:S(2)}, u32[]{:S(2)}) collective-permute-start(bf16[2,284]{1,0:T(2,128)(2,1)S(1)} %slice.265), channel_id=1, source_target_pairs={{0,15},{1,0},{2,1},{3,2},{4,3},{5,4},{6,5},{7,6},{8,7},{9,8},{10,9... | collective-permute-start | bytes 3416 | tf_op jit(solution)/shard_map/ppermute | solution.py:109
  300.4 8.0 %collective-permute-start.39 = (bf16[2,284]{1,0:T(2,128)(2,1)S(1)}, bf16[2,284]{1,0:T(2,128)(2,1)S(1)}, u32[]{:S(2)}, u32[]{:S(2)}) collective-permute-start(bf16[2,284]{1,0:T(2,128)(2,1)S(1)} %collective-permute-done.38), channel_id=1, source_target_pairs={{0,15},{1,0},{2,1},{3,2},{4,3},{5,4},{6,5},{7,6},{8,7},{9,8},{10,9... | collective-permute-start | bytes 3416 | tf_op jit(solution)/shard_map/ppermute | solution.py:109
  303.2 8.0 %collective-permute-start.54 = (bf16[2,284]{1,0:T(2,128)(2,1)S(1)}, bf16[2,284]{1,0:T(2,128)(2,1)S(1)}, u32[]{:S(2)}, u32[]{:S(2)}) collective-permute-start(bf16[2,284]{1,0:T(2,128)(2,1)S(1)} %collective-permute-done.53), channel_id=1, source_target_pairs={{0,15},{1,0},{2,1},{3,2},{4,3},{5,4},{6,5},{7,6},{8,7},{9,8},{10,9... | collective-permute-start | bytes 3416 | tf_op jit(solution)/shard_map/ppermute | solution.py:109
  305.8 5.4 collective-permute-start.1
  305.8 8.9 %collective-permute-start.9 = (bf16[2,284]{1,0:T(2,128)(2,1)S(1)}, bf16[2,284]{1,0:T(2,128)(2,1)S(1)}, u32[]{:S(2)}, u32[]{:S(2)}) collective-permute-start(bf16[2,284]{1,0:T(2,128)(2,1)S(1)} %collective-permute-done.8), channel_id=1, source_target_pairs={{0,15},{1,0},{2,1},{3,2},{4,3},{5,4},{6,5},{7,6},{8,7},{9,8},{10,9... | collective-permute-start | bytes 3416 | tf_op jit(solution)/shard_map/ppermute | solution.py:109
  308.5 6.2 collective-permute-start.16
  308.5 10.7 %collective-permute-start.24 = (bf16[2,284]{1,0:T(2,128)(2,1)S(1)}, bf16[2,284]{1,0:T(2,128)(2,1)S(1)}, u32[]{:S(2)}, u32[]{:S(2)}) collective-permute-start(bf16[2,284]{1,0:T(2,128)(2,1)S(1)} %collective-permute-done.23), channel_id=1, source_target_pairs={{0,15},{1,0},{2,1},{3,2},{4,3},{5,4},{6,5},{7,6},{8,7},{9,8},{10,9... | collective-permute-start | bytes 3416 | tf_op jit(solution)/shard_map/ppermute | solution.py:109
  311.2 8.1 %collective-permute-start.32 = (bf16[2,284]{1,0:T(2,128)(2,1)S(1)}, bf16[2,284]{1,0:T(2,128)(2,1)S(1)}, u32[]{:S(2)}, u32[]{:S(2)}) collective-permute-start(bf16[2,284]{1,0:T(2,128)(2,1)S(1)} %collective-permute-done.31), channel_id=1, source_target_pairs={{0,1},{1,2},{2,3},{3,4},{4,5},{5,6},{6,7},{7,8},{8,9},{9,10},{10,1... | collective-permute-start | bytes 3416 | tf_op jit(solution)/shard_map/ppermute | solution.py:107
  311.2 12.4 %collective-permute-start.40 = (bf16[2,284]{1,0:T(2,128)(2,1)S(1)}, bf16[2,284]{1,0:T(2,128)(2,1)S(1)}, u32[]{:S(2)}, u32[]{:S(2)}) collective-permute-start(bf16[2,284]{1,0:T(2,128)(2,1)S(1)} %collective-permute-done.39), channel_id=1, source_target_pairs={{0,15},{1,0},{2,1},{3,2},{4,3},{5,4},{6,5},{7,6},{8,7},{9,8},{10,9... | collective-permute-start | bytes 3416 | tf_op jit(solution)/shard_map/ppermute | solution.py:109
  314.7 9.0 %collective-permute-start.47 = (bf16[2,284]{1,0:T(2,128)(2,1)S(1)}, bf16[2,284]{1,0:T(2,128)(2,1)S(1)}, u32[]{:S(2)}, u32[]{:S(2)}) collective-permute-start(bf16[2,284]{1,0:T(2,128)(2,1)S(1)} %collective-permute-done.46), channel_id=1, source_target_pairs={{0,1},{1,2},{2,3},{3,4},{4,5},{5,6},{6,7},{7,8},{8,9},{9,10},{10,1... | collective-permute-start | bytes 3416 | tf_op jit(solution)/shard_map/ppermute | solution.py:107
  314.7 13.4 %collective-permute-start.55 = (bf16[2,284]{1,0:T(2,128)(2,1)S(1)}, bf16[2,284]{1,0:T(2,128)(2,1)S(1)}, u32[]{:S(2)}, u32[]{:S(2)}) collective-permute-start(bf16[2,284]{1,0:T(2,128)(2,1)S(1)} %collective-permute-done.54), channel_id=1, source_target_pairs={{0,15},{1,0},{2,1},{3,2},{4,3},{5,4},{6,5},{7,6},{8,7},{9,8},{10,9... | collective-permute-start | bytes 3416 | tf_op jit(solution)/shard_map/ppermute | solution.py:109
  319.2 8.9 %collective-permute-start.2 = (bf16[2,284]{1,0:T(2,128)(2,1)S(1)}, bf16[2,284]{1,0:T(2,128)(2,1)S(1)}, u32[]{:S(2)}, u32[]{:S(2)}) collective-permute-start(bf16[2,284]{1,0:T(2,128)(2,1)S(1)} %collective-permute-done.1), channel_id=1, source_target_pairs={{0,1},{1,2},{2,3},{3,4},{4,5},{5,6},{6,7},{7,8},{8,9},{9,10},{10,1... | collective-permute-start | bytes 3416 | tf_op jit(solution)/shard_map/ppermute | solution.py:107
  319.3 13.3 %collective-permute-start.10 = (bf16[2,284]{1,0:T(2,128)(2,1)S(1)}, bf16[2,284]{1,0:T(2,128)(2,1)S(1)}, u32[]{:S(2)}, u32[]{:S(2)}) collective-permute-start(bf16[2,284]{1,0:T(2,128)(2,1)S(1)} %collective-permute-done.9), channel_id=1, source_target_pairs={{0,15},{1,0},{2,1},{3,2},{4,3},{5,4},{6,5},{7,6},{8,7},{9,8},{10,9... | collective-permute-start | bytes 3416 | tf_op jit(solution)/shard_map/ppermute | solution.py:109
  323.7 9.0 %collective-permute-start.17 = (bf16[2,284]{1,0:T(2,128)(2,1)S(1)}, bf16[2,284]{1,0:T(2,128)(2,1)S(1)}, u32[]{:S(2)}, u32[]{:S(2)}) collective-permute-start(bf16[2,284]{1,0:T(2,128)(2,1)S(1)} %collective-permute-done.16), channel_id=1, source_target_pairs={{0,1},{1,2},{2,3},{3,4},{4,5},{5,6},{6,7},{7,8},{8,9},{9,10},{10,1... | collective-permute-start | bytes 3416 | tf_op jit(solution)/shard_map/ppermute | solution.py:107
  323.7 13.4 %collective-permute-start.25 = (bf16[2,284]{1,0:T(2,128)(2,1)S(1)}, bf16[2,284]{1,0:T(2,128)(2,1)S(1)}, u32[]{:S(2)}, u32[]{:S(2)}) collective-permute-start(bf16[2,284]{1,0:T(2,128)(2,1)S(1)} %collective-permute-done.24), channel_id=1, source_target_pairs={{0,15},{1,0},{2,1},{3,2},{4,3},{5,4},{6,5},{7,6},{8,7},{9,8},{10,9... | collective-permute-start | bytes 3416 | tf_op jit(solution)/shard_map/ppermute | solution.py:109
  328.1 9.0 %collective-permute-start.33 = (bf16[2,284]{1,0:T(2,128)(2,1)S(1)}, bf16[2,284]{1,0:T(2,128)(2,1)S(1)}, u32[]{:S(2)}, u32[]{:S(2)}) collective-permute-start(bf16[2,284]{1,0:T(2,128)(2,1)S(1)} %collective-permute-done.32), channel_id=1, source_target_pairs={{0,1},{1,2},{2,3},{3,4},{4,5},{5,6},{6,7},{7,8},{8,9},{9,10},{10,1... | collective-permute-start | bytes 3416 | tf_op jit(solution)/shard_map/ppermute | solution.py:107
  328.1 13.5 %collective-permute-start.41 = (bf16[2,284]{1,0:T(2,128)(2,1)S(1)}, bf16[2,284]{1,0:T(2,128)(2,1)S(1)}, u32[]{:S(2)}, u32[]{:S(2)}) collective-permute-start(bf16[2,284]{1,0:T(2,128)(2,1)S(1)} %collective-permute-done.40), channel_id=1, source_target_pairs={{0,15},{1,0},{2,1},{3,2},{4,3},{5,4},{6,5},{7,6},{8,7},{9,8},{10,9... | collective-permute-start | bytes 3416 | tf_op jit(solution)/shard_map/ppermute | solution.py:109
  332.6 9.1 %collective-permute-start.48 = (bf16[2,284]{1,0:T(2,128)(2,1)S(1)}, bf16[2,284]{1,0:T(2,128)(2,1)S(1)}, u32[]{:S(2)}, u32[]{:S(2)}) collective-permute-start(bf16[2,284]{1,0:T(2,128)(2,1)S(1)} %collective-permute-done.47), channel_id=1, source_target_pairs={{0,1},{1,2},{2,3},{3,4},{4,5},{5,6},{6,7},{7,8},{8,9},{9,10},{10,1... | collective-permute-start | bytes 3416 | tf_op jit(solution)/shard_map/ppermute | solution.py:107
  332.6 13.5 %collective-permute-start.56 = (bf16[2,284]{1,0:T(2,128)(2,1)S(1)}, bf16[2,284]{1,0:T(2,128)(2,1)S(1)}, u32[]{:S(2)}, u32[]{:S(2)}) collective-permute-start(bf16[2,284]{1,0:T(2,128)(2,1)S(1)} %collective-permute-done.55), channel_id=1, source_target_pairs={{0,15},{1,0},{2,1},{3,2},{4,3},{5,4},{6,5},{7,6},{8,7},{9,8},{10,9... | collective-permute-start | bytes 3416 | tf_op jit(solution)/shard_map/ppermute | solution.py:109
  337.1 9.1 %collective-permute-start.3 = (bf16[2,284]{1,0:T(2,128)(2,1)S(1)}, bf16[2,284]{1,0:T(2,128)(2,1)S(1)}, u32[]{:S(2)}, u32[]{:S(2)}) collective-permute-start(bf16[2,284]{1,0:T(2,128)(2,1)S(1)} %collective-permute-done.2), channel_id=1, source_target_pairs={{0,1},{1,2},{2,3},{3,4},{4,5},{5,6},{6,7},{7,8},{8,9},{9,10},{10,1... | collective-permute-start | bytes 3416 | tf_op jit(solution)/shard_map/ppermute | solution.py:107
  337.1 13.5 %collective-permute-start.11 = (bf16[2,284]{1,0:T(2,128)(2,1)S(1)}, bf16[2,284]{1,0:T(2,128)(2,1)S(1)}, u32[]{:S(2)}, u32[]{:S(2)}) collective-permute-start(bf16[2,284]{1,0:T(2,128)(2,1)S(1)} %collective-permute-done.10), channel_id=1, source_target_pairs={{0,15},{1,0},{2,1},{3,2},{4,3},{5,4},{6,5},{7,6},{8,7},{9,8},{10,9... | collective-permute-start | bytes 3416 | tf_op jit(solution)/shard_map/ppermute | solution.py:109
  341.6 9.0 %collective-permute-start.18 = (bf16[2,284]{1,0:T(2,128)(2,1)S(1)}, bf16[2,284]{1,0:T(2,128)(2,1)S(1)}, u32[]{:S(2)}, u32[]{:S(2)}) collective-permute-start(bf16[2,284]{1,0:T(2,128)(2,1)S(1)} %collective-permute-done.17), channel_id=1, source_target_pairs={{0,1},{1,2},{2,3},{3,4},{4,5},{5,6},{6,7},{7,8},{8,9},{9,10},{10,1... | collective-permute-start | bytes 3416 | tf_op jit(solution)/shard_map/ppermute | solution.py:107
  341.8 13.4 %collective-permute-start.26 = (bf16[2,284]{1,0:T(2,128)(2,1)S(1)}, bf16[2,284]{1,0:T(2,128)(2,1)S(1)}, u32[]{:S(2)}, u32[]{:S(2)}) collective-permute-start(bf16[2,284]{1,0:T(2,128)(2,1)S(1)} %collective-permute-done.25), channel_id=1, source_target_pairs={{0,15},{1,0},{2,1},{3,2},{4,3},{5,4},{6,5},{7,6},{8,7},{9,8},{10,9... | collective-permute-start | bytes 3416 | tf_op jit(solution)/shard_map/ppermute | solution.py:109
  346.1 9.1 %collective-permute-start.34 = (bf16[2,284]{1,0:T(2,128)(2,1)S(1)}, bf16[2,284]{1,0:T(2,128)(2,1)S(1)}, u32[]{:S(2)}, u32[]{:S(2)}) collective-permute-start(bf16[2,284]{1,0:T(2,128)(2,1)S(1)} %collective-permute-done.33), channel_id=1, source_target_pairs={{0,1},{1,2},{2,3},{3,4},{4,5},{5,6},{6,7},{7,8},{8,9},{9,10},{10,1... | collective-permute-start | bytes 3416 | tf_op jit(solution)/shard_map/ppermute | solution.py:107
  346.1 13.5 %collective-permute-start.42 = (bf16[2,284]{1,0:T(2,128)(2,1)S(1)}, bf16[2,284]{1,0:T(2,128)(2,1)S(1)}, u32[]{:S(2)}, u32[]{:S(2)}) collective-permute-start(bf16[2,284]{1,0:T(2,128)(2,1)S(1)} %collective-permute-done.41), channel_id=1, source_target_pairs={{0,15},{1,0},{2,1},{3,2},{4,3},{5,4},{6,5},{7,6},{8,7},{9,8},{10,9... | collective-permute-start | bytes 3416 | tf_op jit(solution)/shard_map/ppermute | solution.py:109
  350.6 9.1 %collective-permute-start.49 = (bf16[2,284]{1,0:T(2,128)(2,1)S(1)}, bf16[2,284]{1,0:T(2,128)(2,1)S(1)}, u32[]{:S(2)}, u32[]{:S(2)}) collective-permute-start(bf16[2,284]{1,0:T(2,128)(2,1)S(1)} %collective-permute-done.48), channel_id=1, source_target_pairs={{0,1},{1,2},{2,3},{3,4},{4,5},{5,6},{6,7},{7,8},{8,9},{9,10},{10,1... | collective-permute-start | bytes 3416 | tf_op jit(solution)/shard_map/ppermute | solution.py:107
  350.6 13.5 %collective-permute-start.57 = (bf16[2,284]{1,0:T(2,128)(2,1)S(1)}, bf16[2,284]{1,0:T(2,128)(2,1)S(1)}, u32[]{:S(2)}, u32[]{:S(2)}) collective-permute-start(bf16[2,284]{1,0:T(2,128)(2,1)S(1)} %collective-permute-done.56), channel_id=1, source_target_pairs={{0,15},{1,0},{2,1},{3,2},{4,3},{5,4},{6,5},{7,6},{8,7},{9,8},{10,9... | collective-permute-start | bytes 3416 | tf_op jit(solution)/shard_map/ppermute | solution.py:109
  355.2 9.1 %collective-permute-start.4 = (bf16[2,284]{1,0:T(2,128)(2,1)S(1)}, bf16[2,284]{1,0:T(2,128)(2,1)S(1)}, u32[]{:S(2)}, u32[]{:S(2)}) collective-permute-start(bf16[2,284]{1,0:T(2,128)(2,1)S(1)} %collective-permute-done.3), channel_id=1, source_target_pairs={{0,1},{1,2},{2,3},{3,4},{4,5},{5,6},{6,7},{7,8},{8,9},{9,10},{10,1... | collective-permute-start | bytes 3416 | tf_op jit(solution)/shard_map/ppermute | solution.py:107
  355.2 13.5 %collective-permute-start.12 = (bf16[2,284]{1,0:T(2,128)(2,1)S(1)}, bf16[2,284]{1,0:T(2,128)(2,1)S(1)}, u32[]{:S(2)}, u32[]{:S(2)}) collective-permute-start(bf16[2,284]{1,0:T(2,128)(2,1)S(1)} %collective-permute-done.11), channel_id=1, source_target_pairs={{0,15},{1,0},{2,1},{3,2},{4,3},{5,4},{6,5},{7,6},{8,7},{9,8},{10,9... | collective-permute-start | bytes 3416 | tf_op jit(solution)/shard_map/ppermute | solution.py:109
  359.6 9.0 %collective-permute-start.19 = (bf16[2,284]{1,0:T(2,128)(2,1)S(1)}, bf16[2,284]{1,0:T(2,128)(2,1)S(1)}, u32[]{:S(2)}, u32[]{:S(2)}) collective-permute-start(bf16[2,284]{1,0:T(2,128)(2,1)S(1)} %collective-permute-done.18), channel_id=1, source_target_pairs={{0,1},{1,2},{2,3},{3,4},{4,5},{5,6},{6,7},{7,8},{8,9},{9,10},{10,1... | collective-permute-start | bytes 3416 | tf_op jit(solution)/shard_map/ppermute | solution.py:107
  359.6 13.5 %collective-permute-start.27 = (bf16[2,284]{1,0:T(2,128)(2,1)S(1)}, bf16[2,284]{1,0:T(2,128)(2,1)S(1)}, u32[]{:S(2)}, u32[]{:S(2)}) collective-permute-start(bf16[2,284]{1,0:T(2,128)(2,1)S(1)} %collective-permute-done.26), channel_id=1, source_target_pairs={{0,15},{1,0},{2,1},{3,2},{4,3},{5,4},{6,5},{7,6},{8,7},{9,8},{10,9... | collective-permute-start | bytes 3416 | tf_op jit(solution)/shard_map/ppermute | solution.py:109
  364.1 9.0 %collective-permute-start.35 = (bf16[2,284]{1,0:T(2,128)(2,1)S(1)}, bf16[2,284]{1,0:T(2,128)(2,1)S(1)}, u32[]{:S(2)}, u32[]{:S(2)}) collective-permute-start(bf16[2,284]{1,0:T(2,128)(2,1)S(1)} %collective-permute-done.34), channel_id=1, source_target_pairs={{0,1},{1,2},{2,3},{3,4},{4,5},{5,6},{6,7},{7,8},{8,9},{9,10},{10,1... | collective-permute-start | bytes 3416 | tf_op jit(solution)/shard_map/ppermute | solution.py:107
  364.3 9.1 %collective-permute-start.43 = (bf16[2,284]{1,0:T(2,128)(2,1)S(1)}, bf16[2,284]{1,0:T(2,128)(2,1)S(1)}, u32[]{:S(2)}, u32[]{:S(2)}) collective-permute-start(bf16[2,284]{1,0:T(2,128)(2,1)S(1)} %collective-permute-done.42), channel_id=1, source_target_pairs={{0,15},{1,0},{2,1},{3,2},{4,3},{5,4},{6,5},{7,6},{8,7},{9,8},{10,9... | collective-permute-start | bytes 3416 | tf_op jit(solution)/shard_map/ppermute | solution.py:109
  368.7 9.1 %collective-permute-start.50 = (bf16[2,284]{1,0:T(2,128)(2,1)S(1)}, bf16[2,284]{1,0:T(2,128)(2,1)S(1)}, u32[]{:S(2)}, u32[]{:S(2)}) collective-permute-start(bf16[2,284]{1,0:T(2,128)(2,1)S(1)} %collective-permute-done.49), channel_id=1, source_target_pairs={{0,1},{1,2},{2,3},{3,4},{4,5},{5,6},{6,7},{7,8},{8,9},{9,10},{10,1... | collective-permute-start | bytes 3416 | tf_op jit(solution)/shard_map/ppermute | solution.py:107
  368.7 9.1 %collective-permute-start.58 = (bf16[2,284]{1,0:T(2,128)(2,1)S(1)}, bf16[2,284]{1,0:T(2,128)(2,1)S(1)}, u32[]{:S(2)}, u32[]{:S(2)}) collective-permute-start(bf16[2,284]{1,0:T(2,128)(2,1)S(1)} %collective-permute-done.57), channel_id=1, source_target_pairs={{0,15},{1,0},{2,1},{3,2},{4,3},{5,4},{6,5},{7,6},{8,7},{9,8},{10,9... | collective-permute-start | bytes 3416 | tf_op jit(solution)/shard_map/ppermute | solution.py:109
  373.1 9.1 %collective-permute-start.5 = (bf16[2,284]{1,0:T(2,128)(2,1)S(1)}, bf16[2,284]{1,0:T(2,128)(2,1)S(1)}, u32[]{:S(2)}, u32[]{:S(2)}) collective-permute-start(bf16[2,284]{1,0:T(2,128)(2,1)S(1)} %collective-permute-done.4), channel_id=1, source_target_pairs={{0,1},{1,2},{2,3},{3,4},{4,5},{5,6},{6,7},{7,8},{8,9},{9,10},{10,1... | collective-permute-start | bytes 3416 | tf_op jit(solution)/shard_map/ppermute | solution.py:107
  373.1 9.1 %collective-permute-start.36 = (bf16[2,284]{1,0:T(2,128)(2,1)S(1)}, bf16[2,284]{1,0:T(2,128)(2,1)S(1)}, u32[]{:S(2)}, u32[]{:S(2)}) collective-permute-start(bf16[2,284]{1,0:T(2,128)(2,1)S(1)} %collective-permute-done.35), channel_id=1, source_target_pairs={{0,1},{1,2},{2,3},{3,4},{4,5},{5,6},{6,7},{7,8},{8,9},{9,10},{10,1... | collective-permute-start | bytes 3416 | tf_op jit(solution)/shard_map/ppermute | solution.py:107
  373.4 9.0 %collective-permute-start.13 = (bf16[2,284]{1,0:T(2,128)(2,1)S(1)}, bf16[2,284]{1,0:T(2,128)(2,1)S(1)}, u32[]{:S(2)}, u32[]{:S(2)}) collective-permute-start(bf16[2,284]{1,0:T(2,128)(2,1)S(1)} %collective-permute-done.12), channel_id=1, source_target_pairs={{0,15},{1,0},{2,1},{3,2},{4,3},{5,4},{6,5},{7,6},{8,7},{9,8},{10,9... | collective-permute-start | bytes 3416 | tf_op jit(solution)/shard_map/ppermute | solution.py:109
  377.7 9.0 %collective-permute-start.20 = (bf16[2,284]{1,0:T(2,128)(2,1)S(1)}, bf16[2,284]{1,0:T(2,128)(2,1)S(1)}, u32[]{:S(2)}, u32[]{:S(2)}) collective-permute-start(bf16[2,284]{1,0:T(2,128)(2,1)S(1)} %collective-permute-done.19), channel_id=1, source_target_pairs={{0,1},{1,2},{2,3},{3,4},{4,5},{5,6},{6,7},{7,8},{8,9},{9,10},{10,1... | collective-permute-start | bytes 3416 | tf_op jit(solution)/shard_map/ppermute | solution.py:107
  377.8 13.4 %collective-permute-start.44 = (bf16[2,284]{1,0:T(2,128)(2,1)S(1)}, bf16[2,284]{1,0:T(2,128)(2,1)S(1)}, u32[]{:S(2)}, u32[]{:S(2)}) collective-permute-start(bf16[2,284]{1,0:T(2,128)(2,1)S(1)} %collective-permute-done.43), channel_id=1, source_target_pairs={{0,15},{1,0},{2,1},{3,2},{4,3},{5,4},{6,5},{7,6},{8,7},{9,8},{10,9... | collective-permute-start | bytes 3416 | tf_op jit(solution)/shard_map/ppermute | solution.py:109
  382.2 9.0 %collective-permute-start.51 = (bf16[2,284]{1,0:T(2,128)(2,1)S(1)}, bf16[2,284]{1,0:T(2,128)(2,1)S(1)}, u32[]{:S(2)}, u32[]{:S(2)}) collective-permute-start(bf16[2,284]{1,0:T(2,128)(2,1)S(1)} %collective-permute-done.50), channel_id=1, source_target_pairs={{0,1},{1,2},{2,3},{3,4},{4,5},{5,6},{6,7},{7,8},{8,9},{9,10},{10,1... | collective-permute-start | bytes 3416 | tf_op jit(solution)/shard_map/ppermute | solution.py:107
  382.2 9.1 %collective-permute-start.37 = (bf16[2,284]{1,0:T(2,128)(2,1)S(1)}, bf16[2,284]{1,0:T(2,128)(2,1)S(1)}, u32[]{:S(2)}, u32[]{:S(2)}) collective-permute-start(bf16[2,284]{1,0:T(2,128)(2,1)S(1)} %collective-permute-done.36), channel_id=1, source_target_pairs={{0,1},{1,2},{2,3},{3,4},{4,5},{5,6},{6,7},{7,8},{8,9},{9,10},{10,1... | collective-permute-start | bytes 3416 | tf_op jit(solution)/shard_map/ppermute | solution.py:107
  382.3 9.4 %collective-permute-start.28 = (bf16[2,284]{1,0:T(2,128)(2,1)S(1)}, bf16[2,284]{1,0:T(2,128)(2,1)S(1)}, u32[]{:S(2)}, u32[]{:S(2)}) collective-permute-start(bf16[2,284]{1,0:T(2,128)(2,1)S(1)} %collective-permute-done.27), channel_id=1, source_target_pairs={{0,15},{1,0},{2,1},{3,2},{4,3},{5,4},{6,5},{7,6},{8,7},{9,8},{10,9... | collective-permute-start | bytes 3416 | tf_op jit(solution)/shard_map/ppermute | solution.py:109
  386.8 9.5 %collective-permute-start.59 = (bf16[2,284]{1,0:T(2,128)(2,1)S(1)}, bf16[2,284]{1,0:T(2,128)(2,1)S(1)}, u32[]{:S(2)}, u32[]{:S(2)}) collective-permute-start(bf16[2,284]{1,0:T(2,128)(2,1)S(1)} %collective-permute-done.58), channel_id=1, source_target_pairs={{0,15},{1,0},{2,1},{3,2},{4,3},{5,4},{6,5},{7,6},{8,7},{9,8},{10,9... | collective-permute-start | bytes 3416 | tf_op jit(solution)/shard_map/ppermute | solution.py:109
  391.2 9.5 %collective-permute-start.6 = (bf16[2,284]{1,0:T(2,128)(2,1)S(1)}, bf16[2,284]{1,0:T(2,128)(2,1)S(1)}, u32[]{:S(2)}, u32[]{:S(2)}) collective-permute-start(bf16[2,284]{1,0:T(2,128)(2,1)S(1)} %collective-permute-done.5), channel_id=1, source_target_pairs={{0,1},{1,2},{2,3},{3,4},{4,5},{5,6},{6,7},{7,8},{8,9},{9,10},{10,1... | collective-permute-start | bytes 3416 | tf_op jit(solution)/shard_map/ppermute | solution.py:107
  391.2 9.5 %collective-permute-start.21 = (bf16[2,284]{1,0:T(2,128)(2,1)S(1)}, bf16[2,284]{1,0:T(2,128)(2,1)S(1)}, u32[]{:S(2)}, u32[]{:S(2)}) collective-permute-start(bf16[2,284]{1,0:T(2,128)(2,1)S(1)} %collective-permute-done.20), channel_id=1, source_target_pairs={{0,1},{1,2},{2,3},{3,4},{4,5},{5,6},{6,7},{7,8},{8,9},{9,10},{10,1... | collective-permute-start | bytes 3416 | tf_op jit(solution)/shard_map/ppermute | solution.py:107
  391.3 9.7 %collective-permute-start.52 = (bf16[2,284]{1,0:T(2,128)(2,1)S(1)}, bf16[2,284]{1,0:T(2,128)(2,1)S(1)}, u32[]{:S(2)}, u32[]{:S(2)}) collective-permute-start(bf16[2,284]{1,0:T(2,128)(2,1)S(1)} %collective-permute-done.51), channel_id=1, source_target_pairs={{0,1},{1,2},{2,3},{3,4},{4,5},{5,6},{6,7},{7,8},{8,9},{9,10},{10,1... | collective-permute-start | bytes 3416 | tf_op jit(solution)/shard_map/ppermute | solution.py:107
  391.8 11.7 %collective-permute-start.14 = (bf16[2,284]{1,0:T(2,128)(2,1)S(1)}, bf16[2,284]{1,0:T(2,128)(2,1)S(1)}, u32[]{:S(2)}, u32[]{:S(2)}) collective-permute-start(bf16[2,284]{1,0:T(2,128)(2,1)S(1)} %collective-permute-done.13), channel_id=1, source_target_pairs={{0,15},{1,0},{2,1},{3,2},{4,3},{5,4},{6,5},{7,6},{8,7},{9,8},{10,9... | collective-permute-start | bytes 3416 | tf_op jit(solution)/shard_map/ppermute | solution.py:109
  396.3 10.2 %collective-permute-start.29 = (bf16[2,284]{1,0:T(2,128)(2,1)S(1)}, bf16[2,284]{1,0:T(2,128)(2,1)S(1)}, u32[]{:S(2)}, u32[]{:S(2)}) collective-permute-start(bf16[2,284]{1,0:T(2,128)(2,1)S(1)} %collective-permute-done.28), channel_id=1, source_target_pairs={{0,15},{1,0},{2,1},{3,2},{4,3},{5,4},{6,5},{7,6},{8,7},{9,8},{10,9... | collective-permute-start | bytes 3416 | tf_op jit(solution)/shard_map/ppermute | solution.py:109
  400.7 5.7 collective-permute-start.7
  400.7 6.0 collective-permute-start.22
  (53 other events, 2449.4 us)
Sparse Core Ops, SparseCore 0:
  9.6 40.6 all-gather.35
  51.8 39.3 all-gather.33
  92.8 22.6 all-gather.27
  116.9 129.3 all-gather.29
  247.6 129.3 all-gather.31
  689.8 90.2 all-reduce.6
